TPU v7x, 256 devices: a whole 4x4x8 slice. The times are simulated.
256 devices in a mesh: row: 32 (over z, x_lo, core), col: 8 (over y, x_hi).
Axes of the slice: x: 4 (x_hi: 2, x_lo: 2; x = x_hi * 2 + x_lo), y: 4, z: 8, core: 2. Of those that a mesh axis runs over, the one named last changes fastest.
Arguments:
- grad_out: bfloat16 [4096, 8192], P('row', 'col'), may hold values from -6 to 6
- weight: bfloat16 [28672, 8192], P('row', 'col'), may hold values from -0.0625 to 0.0625
Outputs:
- grad_in: bfloat16 [4096, 28672], P('col', 'row')
All inputs are finite; a program needn't handle non-finite values.
Results may differ from a plain program's by a relative error of at most 0.015.
Values may be sent and summed in bfloat16 or wider, within the bound.
No kernel may reach another device: no remote copies, remote signals or barrier semaphores. Data moves between devices by JAX's collectives and lax.ppermute only.
A program may use at most 128 MiB of HBM per device.

v0:
```python
import jax
import jax.numpy as jnp
from jax import lax
from jax.sharding import Mesh, PartitionSpec as P


def contract_last(left_side, right_side):
    return lax.dot_general(
        left_side, right_side, (((1,), (1,)), ((), ())), preferred_element_type=jnp.float32
    )


def body(grad_out, weight):
    n_col = lax.axis_size("col")
    n_core = lax.axis_size("core")
    both = lax.all_gather(weight, "core", axis=0, tiled=True)
    gathered = lax.all_gather(grad_out, "rz", axis=0, tiled=True)
    rounded = contract_last(gathered, both).astype(jnp.bfloat16)
    blocks = rounded.reshape(n_col, rounded.shape[0] // n_col, rounded.shape[1])
    received = lax.all_to_all(blocks, "col", 0, 0, tiled=True)
    summed = received.astype(jnp.float32).sum(0).astype(jnp.bfloat16)
    rows, width = (summed.shape[0], weight.shape[0])
    by_owner = summed.reshape(rows, n_core, width).transpose(1, 0, 2)
    mine = lax.all_to_all(by_owner, "core", 0, 0, tiled=True)
    per_row = grad_out.shape[0]
    mine = mine.reshape(n_core, rows // per_row, per_row, width).transpose(1, 0, 2, 3)
    return mine.reshape(-1, width)


def solution(mesh):
    n_row, n_col = mesh.devices.shape
    fine = Mesh(mesh.devices.reshape(n_row // 2, 2, n_col), ("rz", "core", "col"))
    in_specs = (P(("rz", "core"), "col"), P(("rz", "core"), "col"))
    out_specs = P("col", ("rz", "core"))
    return jax.shard_map(body, mesh=fine, in_specs=in_specs, out_specs=out_specs, check_vma=False)
```

profile of v0, /device:TPU:1, one launch (start us, length us, event | category | flops | bytes accessed | tf_op | source)
XLA Modules:
  0.0 252.7 jit_solution(3287596444993253392)
XLA Ops:
  6.5 0.0 all-gather.5.cloned.1.call-start
  6.5 0.7 all-gather.5.cloned.1.call-update
  7.3 0.0 all-gather.3.cloned.1.call-start
  7.3 0.7 all-gather.3.cloned.1.call-update
  8.0 23.9 %all-gather.5.cloned.1.call-done = bf16[1792,1024]{1,0:T(8,128)(2,1)} async-done(((bf16[896,1024]{1,0:T(8,128)(2,1)}), bf16[1792,1024]{1,0:T(8,128)(2,1)}) %all-gather.5.cloned.1.call-update) | async-done | bytes 3670032 | tf_op jit(solution)/shard_map/all_gather | solution.py:16
  31.9 99.0 %all-gather.3.cloned.1.call-done = bf16[2048,1024]{1,0:T(8,128)(2,1)} async-done(((bf16[128,1024]{1,0:T(8,128)(2,1)}), bf16[2048,1024]{1,0:T(8,128)(2,1)}) %all-gather.3.cloned.1.call-update) | async-done | bytes 4194320 | tf_op jit(solution)/shard_map/all_gather | solution.py:17
  131.0 10.7 %convolution_convert_fusion = bf16[2048,1792]{1,0:T(8,128)(2,1)S(1)} fusion(bf16[2048,1024]{1,0:T(8,128)(2,1)} %all-gather.3.cloned.1.call-done, bf16[1792,1024]{1,0:T(8,128)(2,1)} %all-gather.5.cloned.1.call-done), kind=kOutput, calls=%fused_computation | convolution fusion | flops 7519862784 | bytes 15204352 | tf_op jit(solution)/shard_map/dot_general | solution.py:8
  141.6 90.8 %all_to_all.10 = bf16[8,256,1792]{2,1,0:T(8,128)(2,1)} all-to-all(bf16[8,256,1792]{2,1,0:T(8,128)(2,1)S(1)} %bitcast.10), channel_id=1, replica_groups=mesh['rz'=16,'core'=2,'col'=8] {'col'}, dimensions={0} | all-to-all | bytes 14680064 | tf_op jit(solution)/shard_map/all_to_all | solution.py:20
  232.5 4.6 %reduce_sum.12 = bf16[256,1792]{1,0:T(8,128)(2,1)S(1)} reduce(bf16[8,256,1792]{2,1,0:T(8,128)(2,1)} %all_to_all.10, bf16[]{:T(256)} %constant.2.clone.1), dimensions={0}, to_apply=%region_0.0 | reduce | flops 3211264 | bytes 8257538 | tf_op jit(solution)/shard_map/reduce_sum | solution.py:21
  237.1 0.5 copy.5
  237.6 6.6 %all_to_all.11 = bf16[2,256,896]{1,2,0:T(8,128)(2,1)S(1)} all-to-all(bf16[2,256,896]{1,2,0:T(8,128)(2,1)S(1)} %bitcast.11), channel_id=1, replica_groups=mesh['rz'=16,'core'=2,'col'=8] {'core'}, dimensions={0} | all-to-all | bytes 1835008 | tf_op jit(solution)/shard_map/all_to_all | solution.py:24
  244.2 0.6 copy.6
  244.8 1.0 copy.7
Async XLA Ops:
  6.5 25.4 %all-gather.5.cloned.1.call-start = ((), (), s32[]{:S(2)}) async-start(), calls=%async_computation.3 | async-start | bytes 5505024 | tf_op jit(solution)/shard_map/all_gather | solution.py:16
  7.3 123.7 %all-gather.3.cloned.1.call-start = ((), (), s32[]{:S(2)}) async-start(), calls=%async_computation.2 | async-start | bytes 4456448 | tf_op jit(solution)/shard_map/all_gather | solution.py:17
Sparse Core Ops, SparseCore 0:
  9.1 22.7 all-gather.4
  33.7 97.2 all-gather.2
where the time goes:
time: 253 us
  waiting for transfers between devices  124 us (49%)
  blocking collectives  97.5 us (39%)
  between operations  13.4 us (5%)
  matrix products  10.7 us (4%)
  other arithmetic  4.59 us (2%)
    all_gather x1, waiting for transfers between devices, body(): gathered = lax.all_gather(grad_out, 'rz', axis=0, tiled=True)  99 us
    all_to_all x1, blocking collectives, body(): received = lax.all_to_all(blocks, 'col', 0, 0, tiled=True)  90.8 us
    all_gather x1, waiting for transfers between devices, body(): both = lax.all_gather(weight, 'core', axis=0, tiled=True)  23.9 us
    dot_general x1, matrix products, contract_last(): lax.dot_general(left_side, right_side, (((1,), (1,)), ((), ())), preferre...  10.7 us
    all_to_all x1, blocking collectives, body(): mine = lax.all_to_all(by_owner, 'core', 0, 0, tiled=True)  6.62 us
  transfers between devices with their start and end apart: 2, of which 2 were waited for; matrix products, arithmetic and copies ran while one was open for 0% of the time, Pallas kernels for 0%

commit v1 on v0

--- a/solution.py
+++ b/solution.py
@@ -13,7 +13,9 @@
 def body(grad_out, weight):
     n_col = lax.axis_size("col")
     n_core = lax.axis_size("core")
-    both = lax.all_gather(weight, "core", axis=0, tiled=True)
+    both = jnp.concatenate(
+        lax.all_to_all(jnp.stack([weight] * lax.axis_size("core")), "core", 0, 0), axis=0
+    )
     gathered = lax.all_gather(grad_out, "rz", axis=0, tiled=True)
     rounded = contract_last(gathered, both).astype(jnp.bfloat16)
     blocks = rounded.reshape(n_col, rounded.shape[0] // n_col, rounded.shape[1])

time: 253 us -> 237 us (0.937)
  waiting for transfers between devices: 124 us -> 90.1 us
  blocking collectives: 97.5 us -> 108 us
  local copies, waits for them, and re-layouts: 2.12 us -> 5.14 us
    all_gather x1 -> x0, waiting for transfers between devices: 23.9 us -> none  [body(): both = lax.all_gather(weight, 'core', axis=0, tiled=True)]
    all_to_all x0 -> x1, blocking collectives: none -> 10.6 us  [body(): lax.all_to_all(jnp.stack([weight] * lax.axis_size('core')), 'core', 0, 0)]
    all_gather x1, waiting for transfers between devices: 99 us -> 89.3 us  [body(): gathered = lax.all_gather(grad_out, 'rz', axis=0, tiled=True)]
    reshape x0 -> x1, local copies, waits for them, and re-layouts: none -> 3.55 us  [body(): blocks = rounded.reshape(n_col, rounded.shape[0] // n_col, rounded.shape[1])]
  transfers between devices with their start and end apart: 2 -> 1, of which waited for: 2 -> 1; matrix products, arithmetic and copies ran while one was open for 0% -> 1% of each run, Pallas kernels for 0% -> 0%
where the time goes in v1:
time: 237 us; the launch traced here: 236 us
  blocking collectives  108 us (46%)
  waiting for transfers between devices  90.1 us (38%)
  between operations  13.4 us (6%)
  matrix products  12.6 us (5%)
  other arithmetic  7.05 us (3%)
  local copies, waits for them, and re-layouts  5.14 us (2%)
    all_to_all x1, blocking collectives, body(): received = lax.all_to_all(blocks, 'col', 0, 0, tiled=True)  90.8 us
    all_gather x1, waiting for transfers between devices, body(): gathered = lax.all_gather(grad_out, 'rz', axis=0, tiled=True)  89.3 us
    dot_general x1, matrix products, contract_last(): lax.dot_general(left_side, right_side, (((1,), (1,)), ((), ())), preferre...  12.6 us
    all_to_all x1, blocking collectives, body(): lax.all_to_all(jnp.stack([weight] * lax.axis_size('core')), 'core', 0, 0)  10.6 us
    all_to_all x1, blocking collectives, body(): mine = lax.all_to_all(by_owner, 'core', 0, 0, tiled=True)  6.62 us
  transfers between devices with their start and end apart: 1, of which 1 were waited for; matrix products, arithmetic and copies ran while one was open for 1% of the time, Pallas kernels for 0%

profile of v1, /device:TPU:1, one launch (start us, length us, event | category | flops | bytes accessed | tf_op | source)
XLA Modules:
  0.0 236.3 jit_solution(15932079477567392067)
XLA Ops:
  6.5 0.0 all-gather.2.cloned.1.call-start
  6.5 0.7 all-gather.2.cloned.1.call-update
  7.3 2.4 %pad_maximum_fusion = bf16[2,896,1024]{2,1,0:T(8,128)(2,1)S(1)} fusion(bf16[1,896,1024]{2,1,0:T(8,128)(2,1)} %bitcast.21), kind=kLoop, calls=%fused_computation.2 | loop fusion | flops 1835008 | bytes 5505024 | tf_op jit(solution)/shard_map/stack | solution.py:17
  9.6 10.6 %all_to_all.15 = bf16[2,896,1024]{2,1,0:T(8,128)(2,1)} all-to-all(bf16[2,896,1024]{2,1,0:T(8,128)(2,1)S(1)} %pad_maximum_fusion), channel_id=1, replica_groups=mesh['rz'=16,'core'=2,'col'=8] {'core'}, dimensions={0} | all-to-all | bytes 7340032 | tf_op jit(solution)/shard_map/all_to_all | solution.py:17
  20.2 89.3 %all-gather.2.cloned.1.call-done = bf16[2048,1024]{1,0:T(8,128)(2,1)} async-done(((bf16[128,1024]{1,0:T(8,128)(2,1)}), bf16[2048,1024]{1,0:T(8,128)(2,1)}) %all-gather.2.cloned.1.call-update) | async-done | bytes 4194320 | tf_op jit(solution)/shard_map/all_gather | solution.py:19
  109.6 12.6 %convolution_convert_fusion = bf16[1792,2048]{1,0:T(8,128)(2,1)} fusion(bf16[1792,1024]{1,0:T(8,128)(2,1)} %bitcast.19, bf16[2048,1024]{1,0:T(8,128)(2,1)} %all-gather.2.cloned.1.call-done), kind=kOutput, calls=%fused_computation | convolution fusion | flops 7519862784 | bytes 15204352 | tf_op jit(solution)/shard_map/dot_general | solution.py:8
  122.2 3.6 %copy.10 = bf16[224,8,8,256]{3,2,0,1:T(8,128)(2,1)S(1)} copy(bf16[224,8,8,256]{3,2,1,0:T(8,128)(2,1)} %bitcast.17) | data formatting | bytes 14680064 | tf_op jit(solution)/shard_map/reshape | solution.py:21
  125.7 90.8 %all_to_all.16 = bf16[8,256,1792]{1,2,0:T(8,128)(2,1)} all-to-all(bf16[8,256,1792]{1,2,0:T(8,128)(2,1)S(1)} %bitcast.16), channel_id=1, replica_groups=mesh['rz'=16,'core'=2,'col'=8] {'col'}, dimensions={0} | all-to-all | bytes 14680064 | tf_op jit(solution)/shard_map/all_to_all | solution.py:22
  216.6 4.7 %reduce_sum.12 = bf16[256,1792]{0,1:T(8,128)(2,1)S(1)} reduce(bf16[8,256,1792]{1,2,0:T(8,128)(2,1)} %all_to_all.16, bf16[]{:T(256)} %constant.2.clone.1), dimensions={0}, to_apply=%region_0.0 | reduce | flops 3211264 | bytes 8257538 | tf_op jit(solution)/shard_map/reduce_sum | solution.py:23
  221.2 6.6 %all_to_all.17 = bf16[2,256,896]{1,2,0:T(8,128)(2,1)S(1)} all-to-all(bf16[2,256,896]{1,2,0:T(8,128)(2,1)S(1)} %bitcast.18), channel_id=1, replica_groups=mesh['rz'=16,'core'=2,'col'=8] {'core'}, dimensions={0} | all-to-all | bytes 1835008 | tf_op jit(solution)/shard_map/all_to_all | solution.py:26
  227.9 0.6 copy.6
  228.5 1.0 copy.7
Async XLA Ops:
  6.5 103.1 %all-gather.2.cloned.1.call-start = ((), (), s32[]{:S(2)}) async-start(), calls=%async_computation.3 | async-start | bytes 4456448 | tf_op jit(solution)/shard_map/all_gather | solution.py:19
Sparse Core Ops, SparseCore 0:
  9.1 100.4 all-gather.1
